TPU v7x, 32 devices: a whole 2x2x4 slice. The times are simulated.
32 devices in a mesh: section: 2 (over core), expert: 8 (over z, y), tensor: 2 (over x).
Axes of the slice: x: 2, y: 2, z: 4, core: 2. Of those that a mesh axis runs over, the one named last changes fastest.
Arguments:
- hidden_in: bfloat16 [1, 1024, 2560], P(None, 'expert', 'tensor'), may hold values from -6 to 6
- segment_ids: int32 [1, 1024], P(None, 'expert'), may hold values from -1 to 7, as said below
- prompt_lengths: int32 [1, 8], replicated, may hold values from 1 to 682, as said below
- expert_choice: int32 [2, 1, 1024, 4], P('section', None, 'expert'), may hold values from 0 to 7, all different within a row; in each aligned block of 128 rows (0 to 127, 128 to 255, ..., all dimensions but the last counted through in order) at most 80 rows name the same one
- attn_gain: float32 [2, 2560], P('section', 'tensor'), may hold values from 0.1 to 1.9
- ffn_gain: float32 [2, 2560], P('section', 'tensor'), may hold values from 0.1 to 1.9
- w_qkv: bfloat16 [2, 2560, 4, 896], P('section', 'expert', 'tensor'), may hold values from -0.125 to 0.125
- w_out: bfloat16 [2, 2560, 2560], P('section', 'expert', 'tensor'), may hold values from -0.125 to 0.125
- w_shared_in: bfloat16 [2, 2560, 2, 3072], P('section', 'expert', None, 'tensor'), may hold values from -0.125 to 0.125
- w_shared_down: bfloat16 [2, 2560, 3072], P('section', 'expert', 'tensor'), may hold values from -0.109375 to 0.109375
- router_weight: float32 [2, 2560, 8], P('section', 'tensor'), may hold values from -0.125 to 0.125
- w_in: bfloat16 [2, 8, 2560, 2, 1536], P('section', 'expert', None, None, 'tensor'), may hold values from -0.125 to 0.125
- w_down: bfloat16 [2, 8, 1536, 2560], P('section', 'expert', 'tensor'), may hold values from -0.15625 to 0.15625
Outputs:
- hidden_states: bfloat16 [2, 1, 1024, 2560], P('section', None, 'expert', 'tensor')
- kv_cache: bfloat16 [2, 1, 1024, 2, 512], P('section', None, 'expert', None, 'tensor')
Inputs may be any that keep to these rules, and one draw needn't show every extreme that they name: segment_ids agree with prompt_lengths: slot s of micro-batch m lies in prompt j where the first j lengths of m sum to at most s and the first j + 1 to more than s; slots past all 8 prompts hold -1. `prompt_lengths`: in every micro-batch exactly one prompt has 682 slots; the 8 lengths sum to at most 1024. `expert_choice`: the 4 entries of a row differ; in each aligned block of 128 rows (section, micro-batch and slot taken together in order) no expert is named by more than 80 rows.
All inputs are finite; a program needn't handle non-finite values.
Results may differ from a plain program's by a relative error of at most 0.02.
Values may be sent and summed in bfloat16 or wider, within the bound.
No kernel may reach another device: no remote copies, remote signals or barrier semaphores. Data moves between devices by JAX's collectives and lax.ppermute only.
A program may use at most 192 MiB of HBM per device.

v0:
```python
import jax
import jax.numpy as jnp
from jax import lax
from jax.sharding import PartitionSpec as P

HD = 128
NORM_EPS = 1e-05
ROPE_BASE = 500000.0


def passed_along(value, axis, steps):
    count = lax.axis_size(axis)
    leading, last = (max(0, -steps), min(count, count - steps))
    return lax.ppermute(value, axis, [(source, source + steps) for source in range(leading, last)])


def rotate_heads(values_in, positions):
    head_width = values_in.shape[-1]
    half_width = head_width // 2
    frequency = ROPE_BASE ** (-(jnp.arange(half_width, dtype=jnp.float32) * (2.0 / head_width)))
    angles = positions[:, None] * frequency[None, :]
    angles = angles.reshape((positions.shape[0],) + (1,) * (values_in.ndim - 2) + (half_width,))
    cosines = jnp.cos(angles)
    sines = jnp.sin(angles)
    first_half = values_in[..., :half_width]
    second_half = values_in[..., half_width:]
    return jnp.concatenate(
        [first_half * cosines - second_half * sines, second_half * cosines + first_half * sines],
        axis=-1,
    )


def norm_rows(values_in, gain_row, model_width):
    widened = values_in.astype(jnp.float32)
    squares = lax.psum(jnp.sum(widened * widened, axis=-1), "tensor")
    return (widened * lax.rsqrt(squares / model_width + NORM_EPS)[:, None] * gain_row).astype(
        jnp.bfloat16
    )


def terms_to_slots(terms):
    by_slot = lax.all_to_all(terms, "expert", split_axis=0, concat_axis=1, tiled=True)
    return lax.psum_scatter(by_slot, "tensor", scatter_dimension=1, tiled=True)


def expert_path(full_rows, w_in_local, w_down_local):
    sources, slot_count, model_width = full_rows.shape
    local_width = w_down_local.shape[0]
    hidden = jnp.dot(
        full_rows.reshape(sources * slot_count, model_width),
        w_in_local.reshape(model_width, 2 * local_width),
        preferred_element_type=jnp.float32,
    )
    activated = (jax.nn.silu(hidden[:, :local_width]) * hidden[:, local_width:]).astype(
        jnp.bfloat16
    )
    partial_value = jnp.dot(activated, w_down_local, preferred_element_type=jnp.float32)
    partial_value = partial_value.reshape(sources, slot_count, model_width)
    summed = lax.psum_scatter(
        partial_value.astype(jnp.bfloat16), "tensor", scatter_dimension=2, tiled=True
    )
    return lax.all_to_all(summed, "expert", split_axis=0, concat_axis=0, tiled=True)


def local(
    hidden_in,
    segment_ids,
    prompt_lengths,
    expert_choice,
    attn_gain,
    ffn_gain,
    w_qkv,
    w_out,
    w_shared_in,
    w_shared_down,
    router_weight,
    w_in,
    w_down,
):
    sections = lax.axis_size("section")
    section_id = lax.axis_index("section")
    experts_count = lax.axis_size("expert")
    expert_id = lax.axis_index("expert")
    micro_count, tokens_dev, columns = hidden_in.shape
    qkv_full = lax.all_gather(w_qkv[0], "expert", axis=0, tiled=True)
    out_local = w_out[0]
    shared_down_local = w_shared_down[0]
    shared_in_cols = lax.all_to_all(
        w_shared_in[0], "expert", split_axis=2, concat_axis=0, tiled=True
    )
    model_width, kv_local, group_cols = qkv_full.shape
    shared_cols = shared_in_cols.shape[2]
    head_width = HD
    group = group_cols // head_width - 2
    scale = head_width ** (-0.5)
    top_count = expert_choice.shape[-1]
    capacity = 5 * tokens_dev * top_count // (4 * experts_count)
    slot_index = expert_id * tokens_dev + jnp.arange(tokens_dev, dtype=jnp.int32)
    w_in_local = w_in[0, 0]
    w_down_local = w_down[0, 0]
    carried_rows = jnp.zeros((tokens_dev, columns), jnp.bfloat16)
    states = jnp.zeros((micro_count, tokens_dev, columns), jnp.bfloat16)
    caches = jnp.zeros((micro_count, tokens_dev, 2, kv_local * head_width), jnp.bfloat16)
    ticks = micro_count + sections - 1
    for tick_index in range(ticks):
        micro_index = jnp.clip(tick_index - section_id, 0, micro_count - 1)
        incoming = jnp.where(
            section_id == 0, hidden_in[min(tick_index, micro_count - 1)], carried_rows
        )
        active = (tick_index - section_id >= 0) & (tick_index - section_id < micro_count)
        segments = segment_ids[micro_index]
        lengths = prompt_lengths[micro_index]
        choices = expert_choice[0, micro_index]
        starts = jnp.cumsum(lengths) - lengths
        member = segments[:, None] == jnp.arange(lengths.shape[0], dtype=jnp.int32)[None, :]
        first_slot = jnp.sum(jnp.where(member, starts[None, :], 0), axis=1)
        positions = jnp.where(segments >= 0, slot_index - first_slot, 0).astype(jnp.float32)
        normed = norm_rows(incoming, attn_gain[0], model_width)
        normed_full = lax.all_gather(normed, "tensor", axis=1, tiled=True)
        projected = jnp.dot(
            normed_full, qkv_full.reshape(model_width, -1), preferred_element_type=jnp.float32
        )
        projected = projected.reshape(tokens_dev, kv_local, group + 2, head_width)
        queries = rotate_heads(projected[:, :, :group], positions).astype(jnp.bfloat16)
        key_rows = rotate_heads(projected[:, :, group], positions).astype(jnp.bfloat16)
        value_rows = projected[:, :, group + 1].astype(jnp.bfloat16)
        cache = jnp.stack(
            [key_rows.reshape(tokens_dev, -1), value_rows.reshape(tokens_dev, -1)], axis=1
        )
        kv_piece = lax.all_gather(cache.reshape(tokens_dev, -1), "expert", axis=0, tiled=True)
        seg_piece = lax.all_gather(segments, "expert", axis=0, tiled=True)
        key_count = kv_piece.shape[0]
        kv_piece = kv_piece.reshape(key_count, 2, kv_local, head_width)
        key_slots = jnp.arange(key_count, dtype=jnp.int32)
        allowed = (segments[:, None] == seg_piece[None, :]) & (segments[:, None] >= 0) & (
            key_slots[None, :] <= slot_index[:, None]
        ) | (key_slots[None, :] == slot_index[:, None])
        scores = (
            jnp.einsum(
                "tagd,nad->tagn", queries, kv_piece[:, 0], preferred_element_type=jnp.float32
            )
            * scale
        )
        weights_full = jnp.where(allowed[:, None, None, :], jnp.exp(scores), 0.0)
        numerator = jnp.einsum(
            "tagn,nad->tagd",
            weights_full.astype(jnp.bfloat16),
            kv_piece[:, 1],
            preferred_element_type=jnp.float32,
        )
        numerator, denominator = (numerator, jnp.sum(weights_full, axis=-1))
        attended = (numerator / denominator[..., None]).astype(jnp.bfloat16).reshape(tokens_dev, -1)
        attended_all = lax.all_gather(attended, "expert", axis=0, tiled=True)
        attn_terms = lax.dot_general(
            attended_all, out_local, (((1,), (1,)), ((), ())), preferred_element_type=jnp.float32
        )
        attn_sum = terms_to_slots(attn_terms.astype(jnp.bfloat16)).astype(jnp.float32)
        after_attn = (incoming.astype(jnp.float32) + attn_sum).astype(jnp.bfloat16)
        moe_in = norm_rows(after_attn, ffn_gain[0], model_width)
        moe_rows = lax.all_gather(moe_in, "tensor", axis=1, tiled=True)
        moe_all = lax.all_gather(moe_rows, "expert", axis=0, tiled=True)
        shared_hidden = jnp.dot(
            moe_all,
            shared_in_cols.reshape(model_width, 2 * shared_cols),
            preferred_element_type=jnp.float32,
        )
        shared_act = (
            jax.nn.silu(shared_hidden[:, :shared_cols]) * shared_hidden[:, shared_cols:]
        ).astype(jnp.bfloat16)
        shared_act = lax.all_gather(shared_act, "expert", axis=1, tiled=True)
        shared_terms = lax.dot_general(
            shared_act,
            shared_down_local,
            (((1,), (1,)), ((), ())),
            preferred_element_type=jnp.float32,
        )
        shared_sum = terms_to_slots(shared_terms.astype(jnp.bfloat16))
        shared_out = lax.optimization_barrier(shared_sum).astype(jnp.float32)
        logits = lax.psum(
            jnp.dot(moe_in.astype(jnp.float32), router_weight[0], precision=lax.Precision.HIGHEST),
            "tensor",
        )
        expert_ids = jnp.arange(logits.shape[1], dtype=jnp.int32)
        picked = jnp.sum(
            jnp.where(choices[:, :, None] == expert_ids[None, None, :], logits[:, None, :], 0.0),
            axis=2,
        )
        raised = jnp.exp(picked)
        gate_weights = raised / jnp.sum(raised, axis=1, keepdims=True)
        flat_choice = choices.reshape(-1)
        onehot = (flat_choice[:, None] == expert_ids[None, :]).astype(jnp.int32)
        slot_rank = jnp.sum(onehot * (jnp.cumsum(onehot, axis=0) - onehot), axis=1)
        slot_ids = flat_choice * capacity + slot_rank
        row_source = jnp.arange(tokens_dev * top_count, dtype=jnp.int32) // top_count
        table = jnp.zeros((experts_count * capacity,), jnp.int32).at[slot_ids].set(row_source)
        filled = jnp.zeros((experts_count * capacity,), jnp.bool_).at[slot_ids].set(True)
        outgoing = jnp.where(filled[:, None], moe_rows[table], jnp.zeros((), jnp.bfloat16))
        outgoing = outgoing.reshape(experts_count, capacity, model_width)
        returned = expert_path(
            lax.all_to_all(outgoing, "expert", split_axis=0, concat_axis=0, tiled=True),
            w_in_local,
            w_down_local,
        )
        combined = returned.reshape(experts_count * capacity, columns)[slot_ids].astype(jnp.float32)
        combined = combined * gate_weights.reshape(-1)[:, None]
        moe_out = jnp.sum(combined.reshape(tokens_dev, top_count, columns), axis=1)
        output = (after_attn.astype(jnp.float32) + shared_out + moe_out).astype(jnp.bfloat16)
        output, cache = (output, cache)
        states = jnp.where(active, states.at[micro_index].set(output), states)
        caches = jnp.where(active, caches.at[micro_index].set(cache), caches)
        if tick_index + 1 < ticks:
            carried_rows = passed_along(output, "section", 1)
    return (states[None], caches[None])


def solution(mesh):
    placed = (
        P(None, "expert", "tensor"),
        P(None, "expert"),
        P(),
        P("section", None, "expert", None),
        P("section", "tensor"),
        P("section", "tensor"),
        P("section", "expert", "tensor", None),
        P("section", "expert", "tensor"),
        P("section", "expert", None, "tensor"),
        P("section", "expert", "tensor"),
        P("section", "tensor", None),
        P("section", "expert", None, None, "tensor"),
        P("section", "expert", "tensor", None),
    )
    return jax.shard_map(
        local,
        mesh=mesh,
        in_specs=placed,
        out_specs=(
            P("section", None, "expert", "tensor"),
            P("section", None, "expert", None, "tensor"),
        ),
        check_vma=False,
    )
```

profile of v0, /device:TPU:0, one launch (start us, length us, event | category | flops | bytes accessed | tf_op | source)
XLA Modules:
  0.0 1169.4 jit_solution(11774944104342150253)
XLA Ops:
  19.0 9.3 all_gather.43
  29.2 118.6 %all-gather.28.cloned.1.call-done = bf16[1,2560,2,896]{3,2,0,1:T(2,128)(2,1)} async-done(((bf16[1,320,2,896]{3,2,0,1:T(2,128)(2,1)}), bf16[1,2560,2,896]{3,2,0,1:T(2,128)(2,1)}) %all-gather.28.cloned.1.call-update) | async-done | bytes 9175056 | tf_op jit(solution)/shard_map/all_gather | solution.py:85
  147.8 23.0 %copy.131 = bf16[1,2560,2,896]{1,3,2,0:T(8,128)(2,1)} copy(bf16[1,2560,2,896]{3,2,0,1:T(2,128)(2,1)} %all-gather.28.cloned.1.call-done) | data formatting | bytes 18350080 | tf_op jit(solution)/shard_map/reshape | solution.py:121
  177.8 17.5 %all-gather.1 = s32[1,1024]{1,0:T(1,128)S(1)} all-gather(s32[1,128]{1,0:T(1,128)S(1)} %copy-done.31), channel_id=3, replica_groups=mesh['section'=2,'expert'=8,'tensor'=2] {'expert'}, dimensions={1}, use_global_device_ids=true | all-gather | bytes 4608 | tf_op jit(solution)/shard_map/all_gather | solution.py:131
  195.6 20.1 %all-gather.12.cloned.1.call-done = bf16[1024,512]{0,1:T(8,128)(2,1)} async-done(((bf16[128,512]{0,1:T(8,128)(2,1)}), bf16[1024,512]{0,1:T(8,128)(2,1)}) %all-gather.12.cloned.1.call-update) | async-done | bytes 1048592 | tf_op jit(solution)/shard_map/all_gather | solution.py:130
  220.1 55.9 %all-gather.14.cloned.1.call-done = bf16[1024,1280]{0,1:T(8,128)(2,1)} async-done(((bf16[128,1280]{0,1:T(8,128)(2,1)}), bf16[1024,1280]{0,1:T(8,128)(2,1)}) %all-gather.14.cloned.1.call-update) | async-done | bytes 2621456 | tf_op jit(solution)/shard_map/all_gather | solution.py:153
  278.9 20.4 %all_to_all.111 = bf16[8,128,320]{1,2,0:T(8,128)(2,1)S(1)} all-to-all(bf16[8,128,320]{1,2,0:T(8,128)(2,1)S(1)} %bitcast.249), channel_id=1, replica_groups=mesh['section'=2,'expert'=8,'tensor'=2] {'expert'}, dimensions={0} | all-to-all | bytes 1310720 | tf_op jit(solution)/shard_map/all_to_all | solution.py:42
  300.5 14.7 %reduce-scatter.7.cloned.1.call-done = bf16[128,1280]{1,0:T(8,128)(2,1)} async-done(((bf16[128,2560]{1,0:T(8,128)(2,1)}), bf16[128,1280]{1,0:T(8,128)(2,1)}) %reduce-scatter.7.cloned.1.call-update) | async-done | bytes 327696 | tf_op jit(solution)/shard_map/reduce_scatter | solution.py:43
  322.3 9.1 all_gather.48
  361.5 86.2 %all-to-all-done.1 = bf16[320,2,1536]{0,1,2:T(2,128)(2,1)} async-done(((bf16[320,2,1536]{0,1,2:T(2,128)(2,1)}), bf16[320,2,1536]{0,1,2:T(2,128)(2,1)}, u32[]{:S(2)}, u32[]{:S(2)}) %all-to-all-start.1) | async-done | bytes 1966112 | tf_op jit(solution)/shard_map/all_to_all | solution.py:88
  458.2 9.5 all-gather.16.cloned.1.call-done
  481.8 69.7 %all-to-all-done.3 = bf16[8,80,2560]{2,1,0:T(8,128)(2,1)} async-done(((bf16[8,80,2560]{2,1,0:T(8,128)(2,1)}), bf16[8,80,2560]{2,1,0:T(8,128)(2,1)}, u32[]{:S(2)}, u32[]{:S(2)}) %all-to-all-start.3) | async-done | bytes 3276832 | tf_op jit(solution)/shard_map/all_to_all | solution.py:200
  574.4 37.9 %reduce-scatter.11.cloned.1.call-done = bf16[8,80,1280]{2,1,0:T(8,128)(2,1)} async-done(((bf16[8,80,2560]{2,1,0:T(8,128)(2,1)}), bf16[8,80,1280]{2,1,0:T(8,128)(2,1)}) %reduce-scatter.11.cloned.1.call-update) | async-done | bytes 1638416 | tf_op jit(solution)/shard_map/reduce_scatter | solution.py:59
  626.7 30.4 %all-to-all-done.4 = bf16[8,80,1280]{2,1,0:T(8,128)(2,1)S(1)} async-done(((bf16[8,80,1280]{2,1,0:T(8,128)(2,1)}), bf16[8,80,1280]{2,1,0:T(8,128)(2,1)S(1)}, u32[]{:S(2)}, u32[]{:S(2)}) %all-to-all-start.4) | async-done | bytes 1638432 | tf_op jit(solution)/shard_map/all_to_all | solution.py:62
  676.1 9.5 all_gather.51
  692.7 38.3 %all-gather.20.cloned.1.call-done = bf16[1024,512]{0,1:T(8,128)(2,1)} async-done(((bf16[128,512]{0,1:T(8,128)(2,1)}), bf16[1024,512]{0,1:T(8,128)(2,1)}) %all-gather.20.cloned.1.call-update) | async-done | bytes 1048592 | tf_op jit(solution)/shard_map/all_gather | solution.py:130
  735.5 55.9 %all-gather.22.cloned.1.call-done = bf16[1024,1280]{0,1:T(8,128)(2,1)} async-done(((bf16[128,1280]{0,1:T(8,128)(2,1)}), bf16[1024,1280]{0,1:T(8,128)(2,1)}) %all-gather.22.cloned.1.call-update) | async-done | bytes 2621456 | tf_op jit(solution)/shard_map/all_gather | solution.py:153
  794.2 20.4 %all_to_all.112 = bf16[8,128,320]{1,2,0:T(8,128)(2,1)S(1)} all-to-all(bf16[8,128,320]{1,2,0:T(8,128)(2,1)S(1)} %bitcast.251), channel_id=1, replica_groups=mesh['section'=2,'expert'=8,'tensor'=2] {'expert'}, dimensions={0} | all-to-all | bytes 1310720 | tf_op jit(solution)/shard_map/all_to_all | solution.py:42
  815.8 14.7 %reduce-scatter.13.cloned.1.call-done = bf16[128,1280]{1,0:T(8,128)(2,1)} async-done(((bf16[128,2560]{1,0:T(8,128)(2,1)}), bf16[128,1280]{1,0:T(8,128)(2,1)}) %reduce-scatter.13.cloned.1.call-update) | async-done | bytes 327696 | tf_op jit(solution)/shard_map/reduce_scatter | solution.py:43
  837.8 9.1 all_gather.54
  862.0 131.4 %all-gather.24.cloned.1.call-done = bf16[1024,2560]{1,0:T(8,128)(2,1)} async-done(((bf16[128,2560]{1,0:T(8,128)(2,1)}), bf16[1024,2560]{1,0:T(8,128)(2,1)}) %all-gather.24.cloned.1.call-update) | async-done | bytes 5242896 | tf_op jit(solution)/shard_map/all_gather | solution.py:161
  1014.7 44.4 %all-gather.26.cloned.1.call-done = bf16[1024,1536]{0,1:T(8,128)(2,1)} async-done(((bf16[1024,192]{0,1:T(8,128)(2,1)}), bf16[1024,1536]{0,1:T(8,128)(2,1)}) %all-gather.26.cloned.1.call-update) | async-done | bytes 3145744 | tf_op jit(solution)/shard_map/all_gather | solution.py:170
  1066.8 37.8 %reduce-scatter.17.cloned.1.call-done = bf16[8,80,1280]{2,1,0:T(8,128)(2,1)} async-done(((bf16[8,80,2560]{2,1,0:T(8,128)(2,1)}), bf16[8,80,1280]{2,1,0:T(8,128)(2,1)}) %reduce-scatter.17.cloned.1.call-update) | async-done | bytes 1638416 | tf_op jit(solution)/shard_map/reduce_scatter | solution.py:59
  1127.2 22.2 %all-to-all-done.8 = bf16[8,80,1280]{2,1,0:T(8,128)(2,1)S(1)} async-done(((bf16[8,80,1280]{2,1,0:T(8,128)(2,1)}), bf16[8,80,1280]{2,1,0:T(8,128)(2,1)S(1)}, u32[]{:S(2)}, u32[]{:S(2)}) %all-to-all-start.8) | async-done | bytes 1638432 | tf_op jit(solution)/shard_map/all_to_all | solution.py:62
  (245 shorter events, 248.5 us)
Async XLA Ops:
  7.2 559.5 %copy-start = (bf16[1,320,1536]{2,1,0:T(8,128)(2,1)S(1)}, bf16[1,320,1536]{2,1,0:T(8,128)(2,1)}, u32[]{:S(2)}) copy-start(bf16[1,320,1536]{2,1,0:T(8,128)(2,1)} %param.30) | copy-start | bytes 2949124
  7.2 140.6 %all-gather.28.cloned.1.call-start = ((), (), s32[]{:S(2)}) async-start(), calls=%async_computation.29 | async-start | bytes 10321920 | tf_op jit(solution)/shard_map/all_gather | solution.py:85
  7.9 207.8 %all-gather.12.cloned.1.call-start = ((), (), s32[]{:S(2)}) async-start(), calls=%async_computation.15 | async-start | bytes 1179648 | tf_op jit(solution)/shard_map/all_gather | solution.py:130
  177.7 98.2 %all-gather.14.cloned.1.call-start = ((), (), s32[]{:S(2)}) async-start(), calls=%async_computation.16 | async-start | bytes 2949120 | tf_op jit(solution)/shard_map/all_gather | solution.py:153
  220.1 95.2 %reduce-scatter.7.cloned.1.call-start = ((), (), s32[]{:S(2)}) async-start(), calls=%async_computation.17 | async-start | bytes 983040 | tf_op jit(solution)/shard_map/reduce_scatter | solution.py:43
  300.4 167.4 %all-gather.16.cloned.1.call-start = ((), (), s32[]{:S(2)}) async-start(), calls=%async_computation.18 | async-start | bytes 5898240 | tf_op jit(solution)/shard_map/all_gather | solution.py:161
  339.9 107.7 %all-to-all-start.1 = ((bf16[320,2,1536]{0,1,2:T(2,128)(2,1)}), bf16[320,2,1536]{0,1,2:T(2,128)(2,1)}, u32[]{:S(2)}, u32[]{:S(2)}) async-start(bf16[320,2,1536]{0,1,2:T(2,128)(2,1)} %bitcast.242), calls=%async_computation.2 | async-start | bytes 4718592 | tf_op jit(solution)/shard_map/all_to_all | solution.py:88
  447.6 104.0 %all-to-all-start.3 = ((bf16[8,80,2560]{2,1,0:T(8,128)(2,1)}), bf16[8,80,2560]{2,1,0:T(8,128)(2,1)}, u32[]{:S(2)}, u32[]{:S(2)}) async-start(bf16[8,80,2560]{2,1,0:T(8,128)(2,1)} %broadcast_select_fusion.1), calls=%async_computation.5 | async-start | bytes 6553600 | tf_op jit(solution)/shard_map/all_to_all | solution.py:200
  452.1 114.5 %all-gather.18.cloned.1.call-start = ((), (), s32[]{:S(2)}) async-start(), calls=%async_computation.19 | async-start | bytes 3538944 | tf_op jit(solution)/shard_map/all_gather | solution.py:170
  474.1 138.2 %reduce-scatter.11.cloned.1.call-start = ((), (), s32[]{:S(2)}) async-start(), calls=%async_computation.21 | async-start | bytes 4915200 | tf_op jit(solution)/shard_map/reduce_scatter | solution.py:59
  570.7 41.6 %all-to-all-start.2 = ((bf16[8,128,320]{1,2,0:T(8,128)(2,1)}), bf16[8,128,320]{1,2,0:T(8,128)(2,1)S(1)}, u32[]{:S(2)}, u32[]{:S(2)}) async-start(bf16[8,128,320]{1,2,0:T(8,128)(2,1)} %bitcast.232), calls=%async_computation.3 | async-start | bytes 1310720 | tf_op jit(solution)/shard_map/all_to_all | solution.py:42
  613.2 43.9 %all-to-all-start.4 = ((bf16[8,80,1280]{2,1,0:T(8,128)(2,1)}), bf16[8,80,1280]{2,1,0:T(8,128)(2,1)S(1)}, u32[]{:S(2)}, u32[]{:S(2)}) async-start(bf16[8,80,1280]{2,1,0:T(8,128)(2,1)} %reduce-scatter.11.cloned.1.call-done), calls=%async_computation.7 | async-start | bytes 3276800 | tf_op jit(solution)/shard_map/all_to_all | solution.py:62
  618.7 48.5 %reduce-scatter.9.cloned.1.call-start = ((), (), s32[]{:S(2)}) async-start(), calls=%async_computation.20 | async-start | bytes 983040 | tf_op jit(solution)/shard_map/reduce_scatter | solution.py:43
  621.0 110.1 %all-gather.20.cloned.1.call-start = ((), (), s32[]{:S(2)}) async-start(), calls=%async_computation.22 | async-start | bytes 1179648 | tf_op jit(solution)/shard_map/all_gather | solution.py:130
  668.3 2.5 collective-permute-start
  692.6 98.8 %all-gather.22.cloned.1.call-start = ((), (), s32[]{:S(2)}) async-start(), calls=%async_computation.23 | async-start | bytes 2949120 | tf_op jit(solution)/shard_map/all_gather | solution.py:153
  735.4 95.1 %reduce-scatter.13.cloned.1.call-start = ((), (), s32[]{:S(2)}) async-start(), calls=%async_computation.24 | async-start | bytes 983040 | tf_op jit(solution)/shard_map/reduce_scatter | solution.py:43
  815.8 177.7 %all-gather.24.cloned.1.call-start = ((), (), s32[]{:S(2)}) async-start(), calls=%async_computation.25 | async-start | bytes 5898240 | tf_op jit(solution)/shard_map/all_gather | solution.py:161
  856.3 143.5 %all-to-all-start.7 = ((bf16[8,80,2560]{2,1,0:T(8,128)(2,1)}), bf16[8,80,2560]{2,1,0:T(8,128)(2,1)}, u32[]{:S(2)}, u32[]{:S(2)}) async-start(bf16[8,80,2560]{2,1,0:T(8,128)(2,1)} %broadcast_select_fusion), calls=%async_computation.12 | async-start | bytes 6553600 | tf_op jit(solution)/shard_map/all_to_all | solution.py:200
  861.8 197.3 %all-gather.26.cloned.1.call-start = ((), (), s32[]{:S(2)}) async-start(), calls=%async_computation.26 | async-start | bytes 3538944 | tf_op jit(solution)/shard_map/all_gather | solution.py:170
  999.8 104.8 %reduce-scatter.17.cloned.1.call-start = ((), (), s32[]{:S(2)}) async-start(), calls=%async_computation.28 | async-start | bytes 4915200 | tf_op jit(solution)/shard_map/reduce_scatter | solution.py:59
  1063.1 41.5 %all-to-all-start.6 = ((bf16[8,128,320]{1,2,0:T(8,128)(2,1)}), bf16[8,128,320]{1,2,0:T(8,128)(2,1)S(1)}, u32[]{:S(2)}, u32[]{:S(2)}) async-start(bf16[8,128,320]{1,2,0:T(8,128)(2,1)} %bitcast.230), calls=%async_computation.10 | async-start | bytes 1310720 | tf_op jit(solution)/shard_map/all_to_all | solution.py:42
  1105.4 43.9 %all-to-all-start.8 = ((bf16[8,80,1280]{2,1,0:T(8,128)(2,1)}), bf16[8,80,1280]{2,1,0:T(8,128)(2,1)S(1)}, u32[]{:S(2)}, u32[]{:S(2)}) async-start(bf16[8,80,1280]{2,1,0:T(8,128)(2,1)} %reduce-scatter.17.cloned.1.call-done), calls=%async_computation.14 | async-start | bytes 3276800 | tf_op jit(solution)/shard_map/all_to_all | solution.py:62
  1111.0 48.4 %reduce-scatter.15.cloned.1.call-start = ((), (), s32[]{:S(2)}) async-start(), calls=%async_computation.27 | async-start | bytes 983040 | tf_op jit(solution)/shard_map/reduce_scatter | solution.py:43
  (37 other events, 839.2 us)
Sparse Core Ops, SparseCore 0:
  10.2 137.5 all-gather.27
  177.9 37.8 all-gather.11
  220.2 55.7 all-gather.13
  300.5 14.6 reduce-scatter.6
  331.5 136.2 all-gather.15
  474.2 92.3 all-gather.17
  569.0 43.3 reduce-scatter.10
  621.8 16.4 reduce-scatter.8
  692.7 38.3 all-gather.19
  735.5 55.7 all-gather.21
  815.9 14.6 reduce-scatter.12
  847.0 146.3 all-gather.23
  999.9 59.0 all-gather.25
  1061.2 43.3 reduce-scatter.16
  1113.8 16.5 reduce-scatter.14
where the time goes:
time: 1180 us; the launch traced here: 1170 us
  waiting for transfers between devices  790 us (67%)
  blocking collectives  126 us (11%)
  local copies, waits for them, and re-layouts  91.7 us (8%)
  matrix products  70 us (6%)
  other arithmetic  40.5 us (3%)
  starting transfers between devices  36.3 us (3%)
  between operations  14.9 us (1%)
    all_gather x2, waiting for transfers between devices, local(): moe_all = lax.all_gather(moe_rows, 'expert', axis=0, tiled=True)  141 us
    all_gather x1, waiting for transfers between devices, local(): qkv_full = lax.all_gather(w_qkv[0], 'expert', axis=0, tiled=True)  119 us
    all_gather x2, waiting for transfers between devices, local(): attended_all = lax.all_gather(attended, 'expert', axis=0, tiled=True)  112 us
    all_to_all x1, waiting for transfers between devices, local(): lax.all_to_all(w_shared_in[0], 'expert', split_axis=2, concat_axis=0, til...  86.2 us
    reduce_scatter x2, waiting for transfers between devices, expert_path(): lax.psum_scatter(partial_value.astype(jnp.bfloat16), 'tensor', scatter_di...  75.7 us
    all_to_all x2, waiting for transfers between devices, local(): lax.all_to_all(outgoing, 'expert', split_axis=0, concat_axis=0, tiled=True)  69.8 us
    all_gather x2, waiting for transfers between devices, local(): lax.all_gather(cache.reshape(tokens_dev, -1), 'expert', axis=0, tiled=True)  58.4 us
    all_to_all x2, waiting for transfers between devices, expert_path(): lax.all_to_all(summed, 'expert', split_axis=0, concat_axis=0, tiled=True)  52.6 us
  transfers between devices with their start and end apart: 23, of which 18 were waited for; matrix products, arithmetic and copies ran while one was open for 11% of the time, Pallas kernels for 0%

commit v1 on v0

--- a/solution.py
+++ b/solution.py
@@ -6,6 +6,17 @@
 HD = 128
 NORM_EPS = 1e-05
 ROPE_BASE = 500000.0
+
+
+def pass_along(value, mesh_axis, along):
+    size = lax.axis_size(mesh_axis)
+    right = [(i, (i + 1) % size) for i in range(size)]
+    blocks = [value]
+    for stride in range(1, size):
+        blocks = [lax.ppermute(blocks[0], mesh_axis, right), *blocks]
+    result = jnp.concatenate(blocks, axis=along)
+    places = (lax.axis_index(mesh_axis) + 1) * blocks[-1].shape[along]
+    return jnp.roll(result, places, axis=along)
 
 
 def passed_along(value, axis, steps):
@@ -158,7 +169,7 @@
         after_attn = (incoming.astype(jnp.float32) + attn_sum).astype(jnp.bfloat16)
         moe_in = norm_rows(after_attn, ffn_gain[0], model_width)
         moe_rows = lax.all_gather(moe_in, "tensor", axis=1, tiled=True)
-        moe_all = lax.all_gather(moe_rows, "expert", axis=0, tiled=True)
+        moe_all = pass_along(moe_rows, "expert", 0)
         shared_hidden = jnp.dot(
             moe_all,
             shared_in_cols.reshape(model_width, 2 * shared_cols),

time: 1180 us -> 1230 us (1.042)
  blocking collectives: 126 us -> 184 us
  waiting for transfers between devices: 790 us -> 759 us
  starting transfers between devices: 36.3 us -> 52.3 us
    ppermute x0 -> x14, waiting for transfers between devices: none -> 226 us  [pass_along(): blocks = [lax.ppermute(blocks[0], mesh_axis, right), *blocks]]
    all_gather x2 -> x0, waiting for transfers between devices: 141 us -> none  [local(): moe_all = lax.all_gather(moe_rows, 'expert', axis=0, tiled=True)]
    all_to_all x1, waiting for transfers between devices: 86.2 us -> 0.01 us  [local(): lax.all_to_all(w_shared_in[0], 'expert', split_axis=2, concat_axis=0, til...]
    all_to_all x2 -> x4, blocking collectives: 40.8 us -> 98.6 us  [terms_to_slots(): lax.all_to_all(terms, 'expert', split_axis=0, concat_axis=1, tiled=True)]
    reduce_scatter x2, waiting for transfers between devices: 75.7 us -> 48.3 us  [expert_path(): lax.psum_scatter(partial_value.astype(jnp.bfloat16), 'tensor', scatter_di...]
    ppermute x0 -> x14, starting transfers between devices: none -> 24 us  [pass_along(): blocks = [lax.ppermute(blocks[0], mesh_axis, right), *blocks]]
    all_to_all x2, waiting for transfers between devices: 69.8 us -> 88.8 us  [local(): lax.all_to_all(outgoing, 'expert', split_axis=0, concat_axis=0, tiled=True)]
    all_gather x2, waiting for transfers between devices: 44.5 us -> 26.5 us  [local(): shared_act = lax.all_gather(shared_act, 'expert', axis=1, tiled=True)]
  transfers between devices with their start and end apart: 23 -> 33, of which waited for: 18 -> 31; matrix products, arithmetic and copies ran while one was open for 11% -> 10% of each run, Pallas kernels for 0% -> 0%
where the time goes in v1:
time: 1230 us; the launch traced here: 1220 us
  waiting for transfers between devices  759 us (62%)
  blocking collectives  184 us (15%)
  local copies, waits for them, and re-layouts  103 us (8%)
  matrix products  67.2 us (5%)
  starting transfers between devices  52.3 us (4%)
  other arithmetic  39.4 us (3%)
  between operations  15 us (1%)
    ppermute x14, waiting for transfers between devices, pass_along(): blocks = [lax.ppermute(blocks[0], mesh_axis, right), *blocks]  226 us
    all_gather x1, waiting for transfers between devices, local(): qkv_full = lax.all_gather(w_qkv[0], 'expert', axis=0, tiled=True)  119 us
    all_gather x2, waiting for transfers between devices, local(): attended_all = lax.all_gather(attended, 'expert', axis=0, tiled=True)  112 us
    all_to_all x4, blocking collectives, terms_to_slots(): lax.all_to_all(terms, 'expert', split_axis=0, concat_axis=1, tiled=True)  98.6 us
    all_to_all x2, waiting for transfers between devices, local(): lax.all_to_all(outgoing, 'expert', split_axis=0, concat_axis=0, tiled=True)  88.8 us
    all_gather x2, waiting for transfers between devices, local(): lax.all_gather(cache.reshape(tokens_dev, -1), 'expert', axis=0, tiled=True)  58.4 us
    reduce_scatter x2, waiting for transfers between devices, expert_path(): lax.psum_scatter(partial_value.astype(jnp.bfloat16), 'tensor', scatter_di...  48.3 us
    reduce_scatter x4, waiting for transfers between devices, terms_to_slots(): return lax.psum_scatter(by_slot, 'tensor', scatter_dimension=1, tiled=True)  42 us
  transfers between devices with their start and end apart: 33, of which 31 were waited for; matrix products, arithmetic and copies ran while one was open for 10% of the time, Pallas kernels for 0%

profile of v1, /device:TPU:0, one launch (start us, length us, event | category | flops | bytes accessed | tf_op | source)
XLA Modules:
  0.0 1221.0 jit_solution(5953045052659183170)
XLA Ops:
  29.2 118.6 %all-gather.22.cloned.1.call-done = bf16[1,2560,2,896]{3,2,0,1:T(2,128)(2,1)} async-done(((bf16[1,320,2,896]{3,2,0,1:T(2,128)(2,1)}), bf16[1,2560,2,896]{3,2,0,1:T(2,128)(2,1)}) %all-gather.22.cloned.1.call-update) | async-done | bytes 9175056 | tf_op jit(solution)/shard_map/all_gather | solution.py:96
  147.8 23.0 %copy.131 = bf16[1,2560,2,896]{1,3,2,0:T(8,128)(2,1)} copy(bf16[1,2560,2,896]{3,2,0,1:T(2,128)(2,1)} %all-gather.22.cloned.1.call-done) | data formatting | bytes 18350080 | tf_op jit(solution)/shard_map/reshape | solution.py:132
  177.8 17.5 %all-gather.1 = s32[1,1024]{1,0:T(1,128)S(1)} all-gather(s32[1,128]{1,0:T(1,128)S(1)} %copy-done.31), channel_id=3, replica_groups=mesh['section'=2,'expert'=8,'tensor'=2] {'expert'}, dimensions={1}, use_global_device_ids=true | all-gather | bytes 4608 | tf_op jit(solution)/shard_map/all_gather | solution.py:142
  195.6 20.1 %all-gather.10.cloned.1.call-done = bf16[1024,512]{0,1:T(8,128)(2,1)} async-done(((bf16[128,512]{0,1:T(8,128)(2,1)}), bf16[1024,512]{0,1:T(8,128)(2,1)}) %all-gather.10.cloned.1.call-update) | async-done | bytes 1048592 | tf_op jit(solution)/shard_map/all_gather | solution.py:141
  220.1 55.9 %all-gather.12.cloned.1.call-done = bf16[1024,1280]{0,1:T(8,128)(2,1)} async-done(((bf16[128,1280]{0,1:T(8,128)(2,1)}), bf16[1024,1280]{0,1:T(8,128)(2,1)}) %all-gather.12.cloned.1.call-update) | async-done | bytes 2621456 | tf_op jit(solution)/shard_map/all_gather | solution.py:164
  278.9 20.4 %all_to_all.111 = bf16[8,128,320]{1,2,0:T(8,128)(2,1)S(1)} all-to-all(bf16[8,128,320]{1,2,0:T(8,128)(2,1)S(1)} %bitcast.245), channel_id=1, replica_groups=mesh['section'=2,'expert'=8,'tensor'=2] {'expert'}, dimensions={0} | all-to-all | bytes 1310720 | tf_op jit(solution)/shard_map/all_to_all | solution.py:53
  350.5 49.5 %collective-permute-done.1 = bf16[128,2560]{1,0:T(8,128)(2,1)S(1)} collective-permute-done((bf16[128,2560]{1,0:T(8,128)(2,1)S(1)}, bf16[128,2560]{1,0:T(8,128)(2,1)S(1)}, u32[]{:S(2)}, u32[]{:S(2)}) %collective-permute-start.1) | collective-permute-done | bytes 655392 | tf_op jit(solution)/shard_map/ppermute | solution.py:16
  400.8 15.8 %collective-permute-done.2 = bf16[128,2560]{1,0:T(8,128)(2,1)} collective-permute-done((bf16[128,2560]{1,0:T(8,128)(2,1)S(1)}, bf16[128,2560]{1,0:T(8,128)(2,1)}, u32[]{:S(2)}, u32[]{:S(2)}) %collective-permute-start.2) | collective-permute-done | bytes 655392 | tf_op jit(solution)/shard_map/ppermute | solution.py:16
  489.5 26.0 %collective-permute-done.6 = bf16[128,2560]{1,0:T(8,128)(2,1)} collective-permute-done((bf16[128,2560]{1,0:T(8,128)(2,1)}, bf16[128,2560]{1,0:T(8,128)(2,1)}, u32[]{:S(2)}, u32[]{:S(2)}) %collective-permute-start.6) | collective-permute-done | bytes 655392 | tf_op jit(solution)/shard_map/ppermute | solution.py:16
  533.9 40.3 %all-to-all-done.3 = bf16[8,80,2560]{2,1,0:T(8,128)(2,1)} async-done(((bf16[8,80,2560]{2,1,0:T(8,128)(2,1)}), bf16[8,80,2560]{2,1,0:T(8,128)(2,1)}, u32[]{:S(2)}, u32[]{:S(2)}) %all-to-all-start.3) | async-done | bytes 3276832 | tf_op jit(solution)/shard_map/all_to_all | solution.py:211
  604.0 30.0 %all_to_all.112 = bf16[8,128,320]{1,2,0:T(8,128)(2,1)} all-to-all(bf16[8,128,320]{1,2,0:T(8,128)(2,1)S(1)} %bitcast.247), channel_id=1, replica_groups=mesh['section'=2,'expert'=8,'tensor'=2] {'expert'}, dimensions={0} | all-to-all | bytes 1310720 | tf_op jit(solution)/shard_map/all_to_all | solution.py:53
  634.0 24.2 %reduce-scatter.11.cloned.1.call-done = bf16[8,80,1280]{2,1,0:T(8,128)(2,1)} async-done(((bf16[8,80,2560]{2,1,0:T(8,128)(2,1)}), bf16[8,80,1280]{2,1,0:T(8,128)(2,1)}) %reduce-scatter.11.cloned.1.call-update) | async-done | bytes 1638416 | tf_op jit(solution)/shard_map/reduce_scatter | solution.py:70
  683.3 18.8 %all-to-all-done.4 = bf16[8,80,1280]{2,1,0:T(8,128)(2,1)S(1)} async-done(((bf16[8,80,1280]{2,1,0:T(8,128)(2,1)}), bf16[8,80,1280]{2,1,0:T(8,128)(2,1)S(1)}, u32[]{:S(2)}, u32[]{:S(2)}) %all-to-all-start.4) | async-done | bytes 1638432 | tf_op jit(solution)/shard_map/all_to_all | solution.py:73
  737.3 38.3 %all-gather.16.cloned.1.call-done = bf16[1024,512]{0,1:T(8,128)(2,1)} async-done(((bf16[128,512]{0,1:T(8,128)(2,1)}), bf16[1024,512]{0,1:T(8,128)(2,1)}) %all-gather.16.cloned.1.call-update) | async-done | bytes 1048592 | tf_op jit(solution)/shard_map/all_gather | solution.py:141
  780.0 55.9 %all-gather.18.cloned.1.call-done = bf16[1024,1280]{0,1:T(8,128)(2,1)} async-done(((bf16[128,1280]{0,1:T(8,128)(2,1)}), bf16[1024,1280]{0,1:T(8,128)(2,1)}) %all-gather.18.cloned.1.call-update) | async-done | bytes 2621456 | tf_op jit(solution)/shard_map/all_gather | solution.py:164
  838.7 20.4 %all_to_all.113 = bf16[8,128,320]{1,2,0:T(8,128)(2,1)S(1)} all-to-all(bf16[8,128,320]{1,2,0:T(8,128)(2,1)S(1)} %bitcast.248), channel_id=1, replica_groups=mesh['section'=2,'expert'=8,'tensor'=2] {'expert'}, dimensions={0} | all-to-all | bytes 1310720 | tf_op jit(solution)/shard_map/all_to_all | solution.py:53
  892.7 15.6 %collective-permute-done.8 = bf16[128,2560]{1,0:T(8,128)(2,1)S(1)} collective-permute-done((bf16[128,2560]{1,0:T(8,128)(2,1)S(1)}, bf16[128,2560]{1,0:T(8,128)(2,1)S(1)}, u32[]{:S(2)}, u32[]{:S(2)}) %collective-permute-start.8) | collective-permute-done | bytes 655392 | tf_op jit(solution)/shard_map/ppermute | solution.py:16
  908.4 16.2 %collective-permute-done.9 = bf16[128,2560]{1,0:T(8,128)(2,1)S(1)} collective-permute-done((bf16[128,2560]{1,0:T(8,128)(2,1)S(1)}, bf16[128,2560]{1,0:T(8,128)(2,1)S(1)}, u32[]{:S(2)}, u32[]{:S(2)}) %collective-permute-start.9) | collective-permute-done | bytes 655392 | tf_op jit(solution)/shard_map/ppermute | solution.py:16
  925.4 15.3 %collective-permute-done.10 = bf16[128,2560]{1,0:T(8,128)(2,1)S(1)} collective-permute-done((bf16[128,2560]{1,0:T(8,128)(2,1)S(1)}, bf16[128,2560]{1,0:T(8,128)(2,1)S(1)}, u32[]{:S(2)}, u32[]{:S(2)}) %collective-permute-start.10) | collective-permute-done | bytes 655392 | tf_op jit(solution)/shard_map/ppermute | solution.py:16
  997.5 18.9 %collective-permute-done.14 = bf16[128,2560]{1,0:T(8,128)(2,1)} collective-permute-done((bf16[128,2560]{1,0:T(8,128)(2,1)}, bf16[128,2560]{1,0:T(8,128)(2,1)}, u32[]{:S(2)}, u32[]{:S(2)}) %collective-permute-start.14) | collective-permute-done | bytes 655392 | tf_op jit(solution)/shard_map/ppermute | solution.py:16
  1024.9 48.5 %all-to-all-done.7 = bf16[8,80,2560]{2,1,0:T(8,128)(2,1)} async-done(((bf16[8,80,2560]{2,1,0:T(8,128)(2,1)}), bf16[8,80,2560]{2,1,0:T(8,128)(2,1)}, u32[]{:S(2)}, u32[]{:S(2)}) %all-to-all-start.7) | async-done | bytes 3276832 | tf_op jit(solution)/shard_map/all_to_all | solution.py:211
  1106.3 27.7 %all_to_all.114 = bf16[8,128,320]{1,2,0:T(8,128)(2,1)} all-to-all(bf16[8,128,320]{1,2,0:T(8,128)(2,1)S(1)} %bitcast.250), channel_id=1, replica_groups=mesh['section'=2,'expert'=8,'tensor'=2] {'expert'}, dimensions={0} | all-to-all | bytes 1310720 | tf_op jit(solution)/shard_map/all_to_all | solution.py:53
  1134.0 24.1 %reduce-scatter.17.cloned.1.call-done = bf16[8,80,1280]{2,1,0:T(8,128)(2,1)} async-done(((bf16[8,80,2560]{2,1,0:T(8,128)(2,1)}), bf16[8,80,1280]{2,1,0:T(8,128)(2,1)}) %reduce-scatter.17.cloned.1.call-update) | async-done | bytes 1638416 | tf_op jit(solution)/shard_map/reduce_scatter | solution.py:70
  1183.4 18.7 %all-to-all-done.8 = bf16[8,80,1280]{2,1,0:T(8,128)(2,1)S(1)} async-done(((bf16[8,80,1280]{2,1,0:T(8,128)(2,1)}), bf16[8,80,1280]{2,1,0:T(8,128)(2,1)S(1)}, u32[]{:S(2)}, u32[]{:S(2)}) %all-to-all-start.8) | async-done | bytes 1638432 | tf_op jit(solution)/shard_map/all_to_all | solution.py:73
  (281 shorter events, 446.3 us)
Async XLA Ops:
  7.2 140.6 %all-gather.22.cloned.1.call-start = ((), (), s32[]{:S(2)}) async-start(), calls=%async_computation.27 | async-start | bytes 10321920 | tf_op jit(solution)/shard_map/all_gather | solution.py:96
  7.9 207.8 %all-gather.10.cloned.1.call-start = ((), (), s32[]{:S(2)}) async-start(), calls=%async_computation.15 | async-start | bytes 1179648 | tf_op jit(solution)/shard_map/all_gather | solution.py:141
  177.8 98.2 %all-gather.12.cloned.1.call-start = ((), (), s32[]{:S(2)}) async-start(), calls=%async_computation.16 | async-start | bytes 2949120 | tf_op jit(solution)/shard_map/all_gather | solution.py:164
  220.1 95.2 %reduce-scatter.7.cloned.1.call-start = ((), (), s32[]{:S(2)}) async-start(), calls=%async_computation.17 | async-start | bytes 983040 | tf_op jit(solution)/shard_map/reduce_scatter | solution.py:54
  330.5 17.3 %collective-permute-start = (bf16[128,2560]{1,0:T(8,128)(2,1)S(1)}, bf16[128,2560]{1,0:T(8,128)(2,1)S(1)}, u32[]{:S(2)}, u32[]{:S(2)}) collective-permute-start(bf16[128,2560]{1,0:T(8,128)(2,1)S(1)} %all_gather.42), channel_id=1, source_target_pairs={{0,2},{2,4},{4,6},{6,8},{8,10},{10,12},{12,14},{14,0},{1,3},{3,5},... | collective-permute-start | bytes 1966088 | tf_op jit(solution)/shard_map/ppermute | solution.py:16
  340.6 123.4 %all-to-all-start.1 = ((bf16[320,2,1536]{0,1,2:T(2,128)(2,1)}), bf16[320,2,1536]{0,1,2:T(2,128)(2,1)}, u32[]{:S(2)}, u32[]{:S(2)}) async-start(bf16[320,2,1536]{0,1,2:T(2,128)(2,1)} %bitcast.238), calls=%async_computation.2 | async-start | bytes 4718592 | tf_op jit(solution)/shard_map/all_to_all | solution.py:99
  347.9 52.1 %collective-permute-start.1 = (bf16[128,2560]{1,0:T(8,128)(2,1)S(1)}, bf16[128,2560]{1,0:T(8,128)(2,1)S(1)}, u32[]{:S(2)}, u32[]{:S(2)}) collective-permute-start(bf16[128,2560]{1,0:T(8,128)(2,1)S(1)} %collective-permute-done), channel_id=1, source_target_pairs={{0,2},{2,4},{4,6},{6,8},{8,10},{10,12},{12,14},{14,0},{1,3},{3,5},... | collective-permute-start | bytes 1966088 | tf_op jit(solution)/shard_map/ppermute | solution.py:16
  431.7 20.8 %collective-permute-start.4 = (bf16[128,2560]{1,0:T(8,128)(2,1)}, bf16[128,2560]{1,0:T(8,128)(2,1)}, u32[]{:S(2)}, u32[]{:S(2)}) collective-permute-start(bf16[128,2560]{1,0:T(8,128)(2,1)} %collective-permute-done.3), channel_id=1, source_target_pairs={{0,2},{2,4},{4,6},{6,8},{8,10},{10,12},{12,14},{14,0},{1,3},{3,5},... | collective-permute-start | bytes 1966088 | tf_op jit(solution)/shard_map/ppermute | solution.py:16
  452.5 25.1 %collective-permute-start.5 = (bf16[128,2560]{1,0:T(8,128)(2,1)}, bf16[128,2560]{1,0:T(8,128)(2,1)}, u32[]{:S(2)}, u32[]{:S(2)}) collective-permute-start(bf16[128,2560]{1,0:T(8,128)(2,1)} %collective-permute-done.4), channel_id=1, source_target_pairs={{0,2},{2,4},{4,6},{6,8},{8,10},{10,12},{12,14},{14,0},{1,3},{3,5},... | collective-permute-start | bytes 1966088 | tf_op jit(solution)/shard_map/ppermute | solution.py:16
  477.6 37.8 %collective-permute-start.6 = (bf16[128,2560]{1,0:T(8,128)(2,1)}, bf16[128,2560]{1,0:T(8,128)(2,1)}, u32[]{:S(2)}, u32[]{:S(2)}) collective-permute-start(bf16[128,2560]{1,0:T(8,128)(2,1)} %collective-permute-done.5), channel_id=1, source_target_pairs={{0,2},{2,4},{4,6},{6,8},{8,10},{10,12},{12,14},{14,0},{1,3},{3,5},... | collective-permute-start | bytes 1966088 | tf_op jit(solution)/shard_map/ppermute | solution.py:16
  484.9 89.2 %all-to-all-start.3 = ((bf16[8,80,2560]{2,1,0:T(8,128)(2,1)}), bf16[8,80,2560]{2,1,0:T(8,128)(2,1)}, u32[]{:S(2)}, u32[]{:S(2)}) async-start(bf16[8,80,2560]{2,1,0:T(8,128)(2,1)} %broadcast_select_fusion.1), calls=%async_computation.5 | async-start | bytes 6553600 | tf_op jit(solution)/shard_map/all_to_all | solution.py:211
  489.4 111.3 %all-gather.14.cloned.1.call-start = ((), (), s32[]{:S(2)}) async-start(), calls=%async_computation.18 | async-start | bytes 3538944 | tf_op jit(solution)/shard_map/all_gather | solution.py:181
  526.0 132.3 %reduce-scatter.11.cloned.1.call-start = ((), (), s32[]{:S(2)}) async-start(), calls=%async_computation.20 | async-start | bytes 4915200 | tf_op jit(solution)/shard_map/reduce_scatter | solution.py:70
  658.2 43.9 %all-to-all-start.4 = ((bf16[8,80,1280]{2,1,0:T(8,128)(2,1)}), bf16[8,80,1280]{2,1,0:T(8,128)(2,1)S(1)}, u32[]{:S(2)}, u32[]{:S(2)}) async-start(bf16[8,80,1280]{2,1,0:T(8,128)(2,1)} %reduce-scatter.11.cloned.1.call-done), calls=%async_computation.7 | async-start | bytes 3276800 | tf_op jit(solution)/shard_map/all_to_all | solution.py:73
  663.7 19.6 %reduce-scatter.9.cloned.1.call-start = ((), (), s32[]{:S(2)}) async-start(), calls=%async_computation.19 | async-start | bytes 983040 | tf_op jit(solution)/shard_map/reduce_scatter | solution.py:54
  666.0 109.6 %all-gather.16.cloned.1.call-start = ((), (), s32[]{:S(2)}) async-start(), calls=%async_computation.21 | async-start | bytes 1179648 | tf_op jit(solution)/shard_map/all_gather | solution.py:141
  737.1 98.7 %all-gather.18.cloned.1.call-start = ((), (), s32[]{:S(2)}) async-start(), calls=%async_computation.22 | async-start | bytes 2949120 | tf_op jit(solution)/shard_map/all_gather | solution.py:164
  779.9 95.1 %reduce-scatter.13.cloned.1.call-start = ((), (), s32[]{:S(2)}) async-start(), calls=%async_computation.23 | async-start | bytes 983040 | tf_op jit(solution)/shard_map/reduce_scatter | solution.py:54
  987.3 29.1 %collective-permute-start.14 = (bf16[128,2560]{1,0:T(8,128)(2,1)}, bf16[128,2560]{1,0:T(8,128)(2,1)}, u32[]{:S(2)}, u32[]{:S(2)}) collective-permute-start(bf16[128,2560]{1,0:T(8,128)(2,1)} %collective-permute-done.13), channel_id=1, source_target_pairs={{0,2},{2,4},{4,6},{6,8},{8,10},{10,12},{12,14},{14,0},{1,3},{3,5},... | collective-permute-start | bytes 1966088 | tf_op jit(solution)/shard_map/ppermute | solution.py:16
  991.2 82.2 %all-to-all-start.7 = ((bf16[8,80,2560]{2,1,0:T(8,128)(2,1)}), bf16[8,80,2560]{2,1,0:T(8,128)(2,1)}, u32[]{:S(2)}, u32[]{:S(2)}) async-start(bf16[8,80,2560]{2,1,0:T(8,128)(2,1)} %broadcast_select_fusion), calls=%async_computation.12 | async-start | bytes 6553600 | tf_op jit(solution)/shard_map/all_to_all | solution.py:211
  997.2 105.8 %all-gather.20.cloned.1.call-start = ((), (), s32[]{:S(2)}) async-start(), calls=%async_computation.24 | async-start | bytes 3538944 | tf_op jit(solution)/shard_map/all_gather | solution.py:181
  1024.9 133.2 %reduce-scatter.17.cloned.1.call-start = ((), (), s32[]{:S(2)}) async-start(), calls=%async_computation.26 | async-start | bytes 4915200 | tf_op jit(solution)/shard_map/reduce_scatter | solution.py:70
  1158.1 43.9 %all-to-all-start.8 = ((bf16[8,80,1280]{2,1,0:T(8,128)(2,1)}), bf16[8,80,1280]{2,1,0:T(8,128)(2,1)S(1)}, u32[]{:S(2)}, u32[]{:S(2)}) async-start(bf16[8,80,1280]{2,1,0:T(8,128)(2,1)} %reduce-scatter.17.cloned.1.call-done), calls=%async_computation.14 | async-start | bytes 3276800 | tf_op jit(solution)/shard_map/all_to_all | solution.py:73
  1163.6 19.7 %reduce-scatter.15.cloned.1.call-start = ((), (), s32[]{:S(2)}) async-start(), calls=%async_computation.25 | async-start | bytes 983040 | tf_op jit(solution)/shard_map/reduce_scatter | solution.py:54
  (47 other events, 1810.6 us)
Sparse Core Ops, SparseCore 0:
  10.2 137.5 all-gather.21
  177.9 37.8 all-gather.9
  220.2 55.7 all-gather.11
  300.6 14.6 reduce-scatter.6
  526.1 74.6 all-gather.13
  602.9 55.2 reduce-scatter.10
  666.8 16.4 reduce-scatter.8
  737.2 38.2 all-gather.15
  780.1 55.7 all-gather.17
  860.4 14.6 reduce-scatter.12
  1025.0 77.9 all-gather.19
  1105.2 52.8 reduce-scatter.16
  1166.8 16.5 reduce-scatter.14
